TPU v7x, 256 devices: a whole 4x4x8 slice. The times are simulated.
256 devices in a mesh: sec: 2 (over y_lo), dp: 8 (over x, y_hi), seq: 16 (over z, core).
Axes of the slice: x: 4, y: 4 (y_hi: 2, y_lo: 2; y = y_hi * 2 + y_lo), z: 8, core: 2. Of those that a mesh axis runs over, the one named last changes fastest.
Arguments:
- hidden: bfloat16 [256, 128, 2560], P(('sec', 'dp', 'seq')), may hold values from -24 to 24
- cond_shift: bfloat16 [256, 2560], P(('sec', 'dp', 'seq')), may hold values from -0.3125 to 0.3125
- cond_scale: bfloat16 [256, 2560], P(('sec', 'dp', 'seq')), may hold values from -1.75 to 1.75
- noisy: bfloat16 [256, 128, 256], P(('sec', 'dp', 'seq')), may hold values from -6 to 6
- noise_level: float32 [256], P(('sec', 'dp', 'seq')), may hold values from 0.2 to 1
- w_out: bfloat16 [2560, 256], replicated, may hold values from -0.125 to 0.125
- w_embed: bfloat16 [256, 2048], replicated, may hold values from -0.375 to 0.375
- w_root: bfloat16 [2, 2048], replicated, may hold values from -0.03125 to 0.03125
- w_qkv: bfloat16 [3, 2048, 2048], P(None, None, 'seq'), may hold values from -0.125 to 0.125
- w_proj: bfloat16 [2048, 512], P('seq'), may hold values from -0.125 to 0.125
- text_table: bfloat16 [49408, 512], P('seq'), may hold values from -6 to 6
- text_ids: int32 [32, 32], replicated, may hold values from 0 to 49407
- prompt_index: int32 [256], P(('sec', 'dp')), may hold values from 0 to 31
- reward_weight: float32 [256], P(('sec', 'dp')), may hold values from 1000 to 4000
Outputs:
- rewards: float32 [256], P(('sec', 'dp'))
- grad_w_out: float32 [2560, 256], P('seq')
- grad_hidden: bfloat16 [256, 128, 2560], P(('sec', 'dp', 'seq'))
All inputs are finite; a program needn't handle non-finite values.
Results may differ from a plain program's by a relative error of at most 0.017.
The roundings to bfloat16 on the way count: a program that leaves them out, or rounds other values in their place, can miss the bound.
Values may be sent and summed in bfloat16 or wider, within the bound.
No kernel may reach another device: no remote copies, remote signals or barrier semaphores. Data moves between devices by JAX's collectives and lax.ppermute only.
A program may use at most 128 MiB of HBM per device.

v0:
```python
import jax
import jax.numpy as jnp
from jax import lax
from jax.sharding import PartitionSpec as P

D_REW = 2048
HEADS = 16
PROMPTS = 32
normalizing_sharpness = 10.0
epsilon = 1e-06
highest = lax.Precision.HIGHEST


def rotate(angle, first, second):
    cosine = jnp.cos(angle)
    sine_term = jnp.sin(angle)
    return (cosine * first + sine_term * second, cosine * second - sine_term * first)


def suffix(values):
    return jnp.sum(values, axis=1, keepdims=True) - jnp.cumsum(values, axis=1)


def local_path(motion):
    spin = motion[..., 0]
    theta = jnp.cumsum(spin, axis=1) - spin
    step_east, step_north = rotate(theta, motion[..., 1], motion[..., 2])
    path_east = jnp.cumsum(step_east, axis=1) - step_east
    path_north = jnp.cumsum(step_north, axis=1) - step_north
    return (theta, path_east, path_north)


def embed(motion, root_east, root_north, w_embed, root_rows):
    emb = jnp.einsum(
        "cfe,ed->cfd", motion.astype(jnp.bfloat16), w_embed, preferred_element_type=jnp.float32
    )
    emb = emb + root_east[..., None] * root_rows[0] + root_north[..., None] * root_rows[1]
    scale_rms = jnp.sqrt(jnp.mean(emb * emb, axis=-1, keepdims=True) + epsilon)
    return (emb / scale_rms, scale_rms)


def unit_rows(vectors):
    length = jnp.sqrt(jnp.sum(vectors * vectors, axis=-1, keepdims=True) + epsilon)
    return (vectors / length, length)


def norm_grad(grad, normed, scale_rms):
    return (grad - normed * jnp.mean(grad * normed, axis=-1, keepdims=True)) / scale_rms


def motion_grad(d_emb, normed_e, scale_rms, motion, theta, embed_rows, root_rows):
    d_unemb = norm_grad(d_emb, normed_e, scale_rms)
    d_embedded = jnp.einsum("cfd,ed->cfe", d_unemb, embed_rows, precision=highest)
    grad_east = suffix(jnp.sum(d_unemb * root_rows[0], axis=-1))
    grad_north = suffix(jnp.sum(d_unemb * root_rows[1], axis=-1))
    vel_east = motion[..., 1]
    vel_north = motion[..., 2]
    d_east, d_north = rotate(-theta, grad_east, grad_north)
    cosine = jnp.cos(theta)
    sine_term = jnp.sin(theta)
    d_theta = grad_east * (cosine * vel_north - sine_term * vel_east) - grad_north * (
        cosine * vel_east + sine_term * vel_north
    )
    d_spin = suffix(d_theta)
    return d_embedded.at[..., 0].add(d_spin).at[..., 1].add(d_east).at[..., 2].add(d_north)


def local(
    hidden,
    cond_shift,
    cond_scale,
    noisy,
    noise_level,
    w_out,
    w_embed,
    w_root,
    w_qkv,
    w_proj,
    text_table,
    text_ids,
    prompt_index,
    reward_weight,
):
    clips_dev = hidden.shape[0]
    ways = lax.axis_size("seq")
    group = clips_dev * ways
    frames = hidden.shape[1]
    width_cols = w_qkv.shape[2]
    head_size = D_REW // HEADS
    heads_dev = width_cols // head_size
    root_rows = w_root.astype(jnp.float32)
    embed_rows = w_embed.astype(jnp.float32)
    vocab_rows = text_table.shape[0]
    local_ids = text_ids - lax.axis_index("seq") * vocab_rows
    inside = (local_ids >= 0) & (local_ids < vocab_rows)
    picked = jnp.take(text_table, jnp.clip(local_ids, 0, vocab_rows - 1), axis=0).astype(
        jnp.float32
    )
    text_part = jnp.sum(jnp.where(inside[..., None], picked, 0.0), axis=1)
    text_raw = lax.psum(text_part, "seq")
    text_unit, text_len = unit_rows(text_raw)
    hidden_f = hidden.astype(jnp.float32)
    centred = hidden_f - jnp.mean(hidden_f, axis=-1, keepdims=True)
    inv_std = lax.rsqrt(jnp.mean(centred * centred, axis=-1, keepdims=True) + epsilon)
    normed_h = centred * inv_std
    gain = 1.0 + cond_scale.astype(jnp.float32)[:, None, :]
    modulated = (normed_h * gain + cond_shift.astype(jnp.float32)[:, None, :]).astype(jnp.bfloat16)
    eps_pred = jnp.einsum("cfd,de->cfe", modulated, w_out, preferred_element_type=jnp.float32)
    level = noise_level[:, None, None]
    x_clean = noisy.astype(jnp.float32) - level * eps_pred
    theta, path_east, path_north = local_path(x_clean)
    normed_e, scale_rms = embed(x_clean, path_east, path_north, w_embed, root_rows)
    projected = jnp.einsum(
        "cfd,jdk->cfjk",
        lax.all_gather(normed_e.astype(jnp.bfloat16), "seq", axis=0, tiled=True),
        w_qkv,
        preferred_element_type=jnp.float32,
    )
    projected = projected.reshape(group, frames, 3, heads_dev, head_size)
    query_unit, query_len = unit_rows(projected[:, :, 0])
    key_unit, key_len = unit_rows(projected[:, :, 1])
    asking_vectors_group = query_unit.astype(jnp.bfloat16)
    lookup_vectors_group = key_unit.astype(jnp.bfloat16)
    value_b = projected[:, :, 2].astype(jnp.bfloat16)
    similarity_table = normalizing_sharpness * jnp.einsum(
        "cfhd,cghd->chfg",
        asking_vectors_group,
        lookup_vectors_group,
        preferred_element_type=jnp.float32,
    )
    expo = jnp.exp(similarity_table)
    focus_probabilities = expo / jnp.sum(expo, axis=-1, keepdims=True)
    attention_b = focus_probabilities.astype(jnp.bfloat16)
    column_mass = jnp.sum(attention_b, axis=2, dtype=jnp.float32)
    value_f = value_b.astype(jnp.float32)
    pooled = jnp.einsum("chg,cghd->chd", column_mass, value_f, precision=highest)
    pooled_b = pooled.astype(jnp.bfloat16).reshape(group, width_cols)
    motion_part = jnp.dot(pooled_b, w_proj, preferred_element_type=jnp.float32)
    motion_emb = lax.psum(motion_part, "seq")
    choose = (prompt_index[:, None] == jnp.arange(PROMPTS)[None, :]).astype(jnp.float32)
    target = jnp.dot(choose, text_unit, precision=highest)
    emb_len = jnp.sqrt(jnp.sum(motion_emb * motion_emb, axis=-1) + epsilon)
    rewards = jnp.sum(motion_emb * target, axis=-1) / emb_len
    d_memb = (
        (-reward_weight)[:, None]
        * (target - rewards[:, None] * motion_emb / emb_len[:, None])
        / emb_len[:, None]
    )
    d_pooled = jnp.dot(d_memb, w_proj.astype(jnp.float32).T, precision=highest).reshape(
        group, heads_dev, head_size
    )
    reduction_dimension = jnp.einsum("chd,cghd->chg", d_pooled, value_f, precision=highest)
    d_value = jnp.transpose(column_mass, (0, 2, 1))[..., None] * d_pooled[:, None]
    pairwise_dot_similarity = jnp.sum(
        focus_probabilities * reduction_dimension[:, :, None, :], axis=-1, keepdims=True
    )
    similarity_derivative = (
        normalizing_sharpness
        * focus_probabilities
        * (reduction_dimension[:, :, None, :] - pairwise_dot_similarity)
    ).astype(jnp.bfloat16)
    d_qu = jnp.einsum(
        "chfg,cghd->cfhd",
        similarity_derivative,
        lookup_vectors_group,
        preferred_element_type=jnp.float32,
    )
    d_ku = jnp.einsum(
        "chfg,cfhd->cghd",
        similarity_derivative,
        asking_vectors_group,
        preferred_element_type=jnp.float32,
    )
    d_query = (d_qu - query_unit * jnp.sum(query_unit * d_qu, axis=-1, keepdims=True)) / query_len
    d_key = (d_ku - key_unit * jnp.sum(key_unit * d_ku, axis=-1, keepdims=True)) / key_len
    d_proj = (
        jnp.stack([d_query, d_key, d_value], axis=2)
        .astype(jnp.bfloat16)
        .reshape(group, frames, 3, width_cols)
    )
    d_emb = lax.psum_scatter(
        jnp.einsum("cfjk,jdk->cfd", d_proj, w_qkv, preferred_element_type=jnp.float32),
        "seq",
        scatter_dimension=0,
        tiled=True,
    )
    d_motion = motion_grad(d_emb, normed_e, scale_rms, x_clean, theta, embed_rows, root_rows)
    d_eps_b = (-level * d_motion).astype(jnp.bfloat16)
    d_mod = jnp.einsum("cfe,de->cfd", d_eps_b, w_out, preferred_element_type=jnp.float32)
    d_norm = d_mod * gain
    grad_hidden = (
        inv_std
        * (
            d_norm
            - jnp.mean(d_norm, axis=-1, keepdims=True)
            - normed_h * jnp.mean(d_norm * normed_h, axis=-1, keepdims=True)
        )
    ).astype(jnp.bfloat16)
    rows_dev = w_out.shape[0] // ways
    grad_term = jnp.einsum("cfd,cfe->de", modulated, d_eps_b, preferred_element_type=jnp.float32)
    grad_total = lax.psum(grad_term, ("sec", "dp", "seq"))
    grad_w_out = lax.dynamic_slice_in_dim(grad_total, lax.axis_index("seq") * rows_dev, rows_dev, 0)
    return (rewards, grad_w_out, grad_hidden)


def solution(mesh):
    placed = (
        P(("sec", "dp", "seq"), None, None),
        P(("sec", "dp", "seq"), None),
        P(("sec", "dp", "seq"), None),
        P(("sec", "dp", "seq"), None, None),
        P(("sec", "dp", "seq")),
        P(),
        P(),
        P(),
        P(None, None, "seq"),
        P("seq", None),
        P("seq", None),
        P(),
        P(("sec", "dp")),
        P(("sec", "dp")),
    )
    return jax.shard_map(
        local,
        mesh=mesh,
        in_specs=placed,
        out_specs=(P(("sec", "dp")), P("seq", None), P(("sec", "dp", "seq"), None, None)),
        check_vma=False,
    )
```

profile of v0, /device:TPU:2, one launch (start us, length us, event | category | flops | bytes accessed | tf_op | source)
XLA Modules:
  0.0 640.3 jit_solution(5430359469314224564)
XLA Ops:
  9.1 5.1 gather_fusion
  14.2 2.3 select_reduce_fusion
  17.3 1.3 convert_reduce_fusion
  18.5 1.4 fusion.22
  20.7 1.8 fusion.24
  26.0 1.7 multiply_reduce_fusion.3
  30.3 88.0 %all-reduce.3.cloned.1.call-done = f32[32,512]{1,0:T(8,128)} async-done(((f32[32,512]{1,0:T(8,128)}), f32[32,512]{1,0:T(8,128)}) %all-reduce.3.cloned.1.call-update) | async-done | bytes 65552 | tf_op jit(solution)/shard_map/psum | solution.py:100
  118.3 1.0 multiply_reduce_fusion.8
  119.8 55.7 %all-gather.3.cloned.1.call-done = bf16[2048,2048]{1,0:T(8,128)(2,1)} async-done(((bf16[128,2048]{1,0:T(8,128)(2,1)}), bf16[2048,2048]{1,0:T(8,128)(2,1)}) %all-gather.3.cloned.1.call-update) | async-done | bytes 8388624 | tf_op jit(solution)/shard_map/all_gather | solution.py:115
  175.5 6.4 convolution_bitcast_fusion.1
  182.1 1.6 fusion.32
  183.9 2.7 convert_reduce_fusion.1
  186.6 2.1 fusion.37
  188.8 47.4 %psum.21 = f32[16,512]{1,0:T(8,128)} all-reduce(f32[16,512]{1,0:T(8,128)S(1)} %fusion.59), channel_id=1, replica_groups=mesh['sec'=2,'dp'=8,'seq'=16] {'seq'}, use_global_device_ids=true, to_apply=%region_10.11 | all-reduce | flops 8192 | bytes 65536 | tf_op jit(solution)/shard_map/psum | solution.py:139
  236.2 1.2 multiply_reduce_fusion.9
  237.5 1.0 fusion.45
  238.8 1.7 fusion.35
  241.5 1.0 copy-done.2
  244.8 8.1 %convolution_bitcast_fusion = f32[16,128,2048]{2,1,0:T(8,128)} fusion(bf16[16,128,1,128]{1,3,0,2:T(8,128)(2,1)S(1)} %multiply_convert_fusion, bf16[16,128,1,128]{1,3,0,2:T(8,128)(2,1)S(1)} %get-tuple-element.60, bf16[16,128,1,128]{1,3,0,2:T(8,128)(2,1)S(1)} %get-tuple-element.59, bf16[3,2048,128]{2,1,0:T(8,128)(2,1)S(1)} %copy-done.9), kind=kOutput, calls=%fused_computation.2 | convolution fusion | flops 3222798336 | bytes 19922944 | tf_op jit(solution)/shard_map/cfjk,jdk->cfd/dot_general | solution.py:182
  253.2 100.2 %reduce-scatter.2.cloned.1.call-done = f32[1,128,2048]{2,1,0:T(8,128)} async-done(((f32[16,128,2048]{2,1,0:T(8,128)}), f32[1,128,2048]{2,1,0:T(8,128)}) %reduce-scatter.2.cloned.1.call-update) | async-done | bytes 1048592 | tf_op jit(solution)/shard_map/reduce_scatter | solution.py:181
  353.5 1.9 fusion.30
  355.7 2.1 multiply_reduce_fusion.7
  358.4 2.0 fusion.66
  360.8 2.7 fusion.27
  363.6 1.3 fusion.40
  364.9 1.0 scatter-add.10
  367.2 3.3 fusion.53
  371.2 3.2 fusion.18
  374.3 1.5 reduce_sum.224
  375.8 2.8 fusion.21
  378.7 253.5 %all-reduce.5.cloned.1.call-done = f32[2560,256]{1,0:T(8,128)} async-done(((f32[2560,256]{1,0:T(8,128)}), f32[2560,256]{1,0:T(8,128)}) %all-reduce.5.cloned.1.call-update) | async-done | bytes 2621456 | tf_op jit(solution)/shard_map/psum | solution.py:201
  632.2 1.6 constant_dynamic-slice_fusion
  (126 shorter events, 16.8 us)
Async XLA Ops:
  7.2 1.9 copy-start
  7.2 111.1 %all-reduce.3.cloned.1.call-start = ((), (), s32[]{:S(2)}) async-start(), calls=%async_computation.1 | async-start | bytes 131072 | tf_op jit(solution)/shard_map/psum | solution.py:100
  14.1 5.8 copy-start.20
  14.1 6.4 %copy-start.21 = (bf16[1,2560]{1,0:T(2,128)(2,1)S(1)}, bf16[1,2560]{1,0:T(2,128)(2,1)}, u32[]{:S(2)}) copy-start(bf16[1,2560]{1,0:T(2,128)(2,1)} %param.21) | copy-start | bytes 15364
  14.1 6.4 %copy-start.22 = (bf16[1,2560]{1,0:T(2,128)(2,1)S(1)}, bf16[1,2560]{1,0:T(2,128)(2,1)}, u32[]{:S(2)}) copy-start(bf16[1,2560]{1,0:T(2,128)(2,1)} %param.22) | copy-start | bytes 15364
  14.2 6.5 %copy-start.36 = (bf16[1,128,256]{2,1,0:T(8,128)(2,1)S(1)}, bf16[1,128,256]{2,1,0:T(8,128)(2,1)}, u32[]{:S(2)}) copy-start(bf16[1,128,256]{2,1,0:T(8,128)(2,1)} %param.23) | copy-start | bytes 196612
  16.5 159.0 %all-gather.3.cloned.1.call-start = ((), (), s32[]{:S(2)}) async-start(), calls=%async_computation.4 | async-start | bytes 8912896 | tf_op jit(solution)/shard_map/all_gather | solution.py:115
  16.5 4.1 copy-start.3
  18.5 3.9 copy-start.23
  20.0 2.5 copy-start.27
  20.7 1.8 copy-start.14
  24.9 2.8 copy-start.10
  27.8 2.0 copy-start.37
  29.7 323.8 %reduce-scatter.2.cloned.1.call-start = ((), (), s32[]{:S(2)}) async-start(), calls=%async_computation.2 | async-start | bytes 17825792 | tf_op jit(solution)/shard_map/reduce_scatter | solution.py:181
  181.9 2.0 copy-start.1
  183.9 4.8 copy-start.13
  183.9 52.3 %copy-start.16 = (f32[32,512]{1,0:T(8,128)S(1)}, f32[32,512]{1,0:T(8,128)}, u32[]{:S(2)}) copy-start(f32[32,512]{1,0:T(8,128)} %all-reduce.3.cloned.1.call-done) | copy-start | bytes 196612
  236.2 4.4 copy-start.6
  237.4 3.5 copy-start.35
  238.4 2.5 copy-start.8
  240.6 1.9 copy-start.2
  253.0 100.5 %copy-start.26 = (f32[128]{0:T(128)S(1)}, f32[128]{0:T(128)}, u32[]{:S(2)}) copy-start(f32[128]{0:T(128)} %copy-done.25) | copy-start | bytes 1540
  253.0 102.5 %copy-start.19 = (f32[1,2048]{1,0:T(1,128)S(1)}, f32[1,2048]{1,0:T(1,128)}, u32[]{:S(2)}) copy-start(f32[1,2048]{1,0:T(1,128)} %get-tuple-element.67) | copy-start | bytes 24580
  253.0 102.5 %copy-start.18 = (f32[1,2048]{1,0:T(1,128)S(1)}, f32[1,2048]{1,0:T(1,128)}, u32[]{:S(2)}) copy-start(f32[1,2048]{1,0:T(1,128)} %get-tuple-element.66) | copy-start | bytes 24580
  253.0 379.2 %all-reduce.5.cloned.1.call-start = ((), (), s32[]{:S(2)}) async-start(), calls=%async_computation.3 | async-start | bytes 5242880 | tf_op jit(solution)/shard_map/psum | solution.py:201
  353.5 2.0 copy-start.5
  353.5 2.2 copy-start.7
  355.6 2.7 copy-start.29
  355.6 2.7 copy-start.30
  355.6 2.7 copy-start.32
  355.6 2.7 copy-start.34
  355.6 5.0 copy-start.11
  (10 other events, 10.1 us)
Sparse Core Ops, SparseCore 0:
  16.6 101.6 all-reduce.2
  120.9 54.6 all-gather.2
  253.1 100.3 reduce-scatter.1
  370.6 261.4 all-reduce.4
where the time goes:
time: 641 us; the launch traced here: 640 us
  waiting for transfers between devices  498 us (78%)
  blocking collectives  47.4 us (7%)
  matrix products  37.3 us (6%)
  other arithmetic  26.9 us (4%)
  local copies, waits for them, and re-layouts  15.9 us (2%)
  between operations  14.9 us (2%)
    psum x1, waiting for transfers between devices, local(): grad_total = lax.psum(grad_term, ('sec', 'dp', 'seq'))  253 us
    reduce_scatter x1, waiting for transfers between devices, local(): lax.psum_scatter(jnp.einsum('cfjk,jdk->cfd', d_proj, w_qkv, preferred_ele...  100 us
    psum x1, waiting for transfers between devices, local(): text_raw = lax.psum(text_part, 'seq')  88 us
    all_gather x1, waiting for transfers between devices, local(): lax.all_gather(normed_e.astype(jnp.bfloat16), 'seq', axis=0, tiled=True)  55.7 us
    psum x1, blocking collectives, local(): motion_emb = lax.psum(motion_part, 'seq')  47.4 us
  transfers between devices with their start and end apart: 4, of which 4 were waited for; matrix products, arithmetic and copies ran while one was open for 3% of the time, Pallas kernels for 0%

commit v1 on v0

--- a/solution.py
+++ b/solution.py
@@ -198,7 +198,7 @@
     ).astype(jnp.bfloat16)
     rows_dev = w_out.shape[0] // ways
     grad_term = jnp.einsum("cfd,cfe->de", modulated, d_eps_b, preferred_element_type=jnp.float32)
-    grad_total = lax.psum(grad_term, ("sec", "dp", "seq"))
+    grad_total = lax.psum(lax.psum(grad_term, ("dp", "seq")), "sec")
     grad_w_out = lax.dynamic_slice_in_dim(grad_total, lax.axis_index("seq") * rows_dev, rows_dev, 0)
     return (rewards, grad_w_out, grad_hidden)
 

time: 641 us -> 1710 us (2.67)
  waiting for transfers between devices: 498 us -> 1560 us
    psum x1 -> x2, waiting for transfers between devices: 253 us -> 1320 us  [local(): grad_total = lax.psum(lax.psum(grad_term, ('dp', 'seq')), 'sec')]
  transfers between devices with their start and end apart: 4 -> 5, of which waited for: 4 -> 5; matrix products, arithmetic and copies ran while one was open for 3% -> 1% of each run, Pallas kernels for 0% -> 0%
where the time goes in v1:
time: 1710 us; the launch traced here: 1700 us
  waiting for transfers between devices  1560 us (91%)
  blocking collectives  47.4 us (3%)
  matrix products  37.3 us (2%)
  other arithmetic  26.9 us (2%)
    psum x2, waiting for transfers between devices, local(): grad_total = lax.psum(lax.psum(grad_term, ('dp', 'seq')), 'sec')  1320 us
    reduce_scatter x1, waiting for transfers between devices, local(): lax.psum_scatter(jnp.einsum('cfjk,jdk->cfd', d_proj, w_qkv, preferred_ele...  100 us
    psum x1, waiting for transfers between devices, local(): text_raw = lax.psum(text_part, 'seq')  88 us
    all_gather x1, waiting for transfers between devices, local(): lax.all_gather(normed_e.astype(jnp.bfloat16), 'seq', axis=0, tiled=True)  55.7 us
    psum x1, blocking collectives, local(): motion_emb = lax.psum(motion_part, 'seq')  47.4 us
  transfers between devices with their start and end apart: 5, of which 5 were waited for; matrix products, arithmetic and copies ran while one was open for 1% of the time, Pallas kernels for 0%

profile of v1, /device:TPU:2, one launch (start us, length us, event | category | flops | bytes accessed | tf_op | source)
XLA Modules:
  0.0 1704.8 jit_solution(3453274820020587486)
XLA Ops:
  9.1 5.1 gather_fusion
  14.2 2.3 select_reduce_fusion
  17.3 1.3 convert_reduce_fusion
  18.5 1.4 fusion.22
  20.7 1.8 fusion.24
  26.0 1.7 multiply_reduce_fusion.3
  30.3 88.0 %all-reduce.4.cloned.1.call-done = f32[32,512]{1,0:T(8,128)} async-done(((f32[32,512]{1,0:T(8,128)}), f32[32,512]{1,0:T(8,128)}) %all-reduce.4.cloned.1.call-update) | async-done | bytes 65552 | tf_op jit(solution)/shard_map/psum | solution.py:100
  119.8 55.7 %all-gather.3.cloned.1.call-done = bf16[2048,2048]{1,0:T(8,128)(2,1)} async-done(((bf16[128,2048]{1,0:T(8,128)(2,1)}), bf16[2048,2048]{1,0:T(8,128)(2,1)}) %all-gather.3.cloned.1.call-update) | async-done | bytes 8388624 | tf_op jit(solution)/shard_map/all_gather | solution.py:115
  175.5 6.4 convolution_bitcast_fusion.1
  182.1 1.6 fusion.32
  183.9 2.7 convert_reduce_fusion.1
  186.6 2.1 fusion.37
  188.9 47.4 %psum.28 = f32[16,512]{1,0:T(8,128)} all-reduce(f32[16,512]{1,0:T(8,128)S(1)} %fusion.59), channel_id=1, replica_groups=mesh['sec'=2,'dp'=8,'seq'=16] {'seq'}, use_global_device_ids=true, to_apply=%region_10.11 | all-reduce | flops 8192 | bytes 65536 | tf_op jit(solution)/shard_map/psum | solution.py:139
  236.3 1.2 multiply_reduce_fusion.9
  237.5 1.0 fusion.45
  238.9 1.7 fusion.35
  241.6 1.0 copy-done.2
  244.9 8.1 convolution_bitcast_fusion
  253.3 100.3 %reduce-scatter.2.cloned.1.call-done = f32[1,128,2048]{2,1,0:T(8,128)} async-done(((f32[16,128,2048]{2,1,0:T(8,128)}), f32[1,128,2048]{2,1,0:T(8,128)}) %reduce-scatter.2.cloned.1.call-update) | async-done | bytes 1048592 | tf_op jit(solution)/shard_map/reduce_scatter | solution.py:181
  353.5 1.9 fusion.30
  355.7 2.1 multiply_reduce_fusion.7
  358.5 2.0 fusion.66
  360.9 2.7 fusion.27
  363.6 1.3 fusion.40
  365.0 1.0 scatter-add.10
  367.3 3.3 fusion.53
  370.6 1175.1 %all-reduce.6.cloned.1.call-done = f32[2560,256]{1,0:T(8,128)} async-done(((f32[2560,256]{1,0:T(8,128)}), f32[2560,256]{1,0:T(8,128)}) %all-reduce.6.cloned.1.call-update) | async-done | bytes 2621456 | tf_op jit(solution)/shard_map/psum | solution.py:201
  1546.5 3.2 fusion.18
  1549.6 1.5 reduce_sum.224
  1551.1 2.8 fusion.21
  1554.0 142.7 %all-reduce.8.cloned.1.call-done = f32[2560,256]{1,0:T(8,128)} async-done(((f32[2560,256]{1,0:T(8,128)}), f32[2560,256]{1,0:T(8,128)}) %all-reduce.8.cloned.1.call-update) | async-done | bytes 2621456 | tf_op jit(solution)/shard_map/psum | solution.py:201
  1696.7 1.6 constant_dynamic-slice_fusion
  (129 shorter events, 17.9 us)
Async XLA Ops:
  7.2 1.9 copy-start
  7.2 111.1 %all-reduce.4.cloned.1.call-start = ((), (), s32[]{:S(2)}) async-start(), calls=%async_computation.1 | async-start | bytes 131072 | tf_op jit(solution)/shard_map/psum | solution.py:100
  14.1 5.8 copy-start.20
  14.1 6.4 copy-start.21
  14.1 6.4 copy-start.22
  14.2 6.5 copy-start.36
  16.5 159.0 %all-gather.3.cloned.1.call-start = ((), (), s32[]{:S(2)}) async-start(), calls=%async_computation.5 | async-start | bytes 8912896 | tf_op jit(solution)/shard_map/all_gather | solution.py:115
  16.5 4.1 copy-start.3
  18.5 3.9 copy-start.23
  20.0 2.5 copy-start.27
  24.9 2.8 copy-start.10
  27.8 2.0 copy-start.37
  29.7 323.8 %reduce-scatter.2.cloned.1.call-start = ((), (), s32[]{:S(2)}) async-start(), calls=%async_computation.2 | async-start | bytes 17825792 | tf_op jit(solution)/shard_map/reduce_scatter | solution.py:181
  181.9 2.0 copy-start.1
  183.9 4.8 copy-start.13
  183.9 52.3 %copy-start.16 = (f32[32,512]{1,0:T(8,128)S(1)}, f32[32,512]{1,0:T(8,128)}, u32[]{:S(2)}) copy-start(f32[32,512]{1,0:T(8,128)} %all-reduce.4.cloned.1.call-done) | copy-start | bytes 196612
  236.3 4.4 copy-start.6
  237.5 3.5 copy-start.35
  238.5 2.5 copy-start.8
  240.6 1.9 copy-start.2
  253.0 100.5 %copy-start.26 = (f32[128]{0:T(128)S(1)}, f32[128]{0:T(128)}, u32[]{:S(2)}) copy-start(f32[128]{0:T(128)} %copy-done.25) | copy-start | bytes 1540
  253.0 102.5 %copy-start.18 = (f32[1,2048]{1,0:T(1,128)S(1)}, f32[1,2048]{1,0:T(1,128)}, u32[]{:S(2)}) copy-start(f32[1,2048]{1,0:T(1,128)} %get-tuple-element.66) | copy-start | bytes 24580
  253.0 102.5 %copy-start.19 = (f32[1,2048]{1,0:T(1,128)S(1)}, f32[1,2048]{1,0:T(1,128)}, u32[]{:S(2)}) copy-start(f32[1,2048]{1,0:T(1,128)} %get-tuple-element.67) | copy-start | bytes 24580
  253.1 1292.7 %all-reduce.6.cloned.1.call-start = ((), (), s32[]{:S(2)}) async-start(), calls=%async_computation.3 | async-start | bytes 5242880 | tf_op jit(solution)/shard_map/psum | solution.py:201
  353.5 2.0 copy-start.5
  353.5 2.2 copy-start.7
  355.7 2.7 copy-start.29
  355.7 2.7 copy-start.30
  355.7 2.7 copy-start.32
  355.7 2.7 copy-start.34
  355.7 5.0 copy-start.11
  370.6 1326.1 %all-reduce.8.cloned.1.call-start = ((), (), s32[]{:S(2)}) async-start(), calls=%async_computation.4 | async-start | bytes 5242880 | tf_op jit(solution)/shard_map/psum | solution.py:201
  (11 other events, 11.9 us)
Sparse Core Ops, SparseCore 0:
  16.6 101.6 all-reduce.3
  120.9 54.6 all-gather.2
  253.2 100.3 reduce-scatter.1
  370.7 1175.0 all-reduce.5
  1548.2 148.4 all-reduce.7
